TPU v7x, 256 devices: a whole 4x4x8 slice. The times are simulated.
256 devices in a mesh: req: 64 (over z, y, core), tp: 4 (over x).
Axes of the slice: x: 4, y: 4, z: 8, core: 2. Of those that a mesh axis runs over, the one named last changes fastest.
Arguments:
- tokens: bfloat16 [32768, 2048], P(('req', 'tp')), may hold values from -1000 to 1000
- query_weight: bfloat16 [2048, 2048], P(None, 'tp'), may hold values from -0.3125 to 0.3125
- kv_weight: bfloat16 [2048, 2, 2048], P(None, None, 'tp'), may hold values from -0.125 to 0.125
- out_weight: bfloat16 [2048, 2048], P('tp'), may hold values from -0.125 to 0.125
- cached_keys: bfloat16 [65536, 2048], P('req', 'tp'), may hold values from -70 to 70
- cached_values: bfloat16 [65536, 2048], P('req', 'tp'), may hold values from -6 to 6
- request_lengths: int32 [32], replicated, may hold values from 1 to 3, 64 in all
- group_order: int32 [64], replicated, may hold values from 0 to 63, each once
- group_offset: int32 [64], replicated, may hold values from 0 to 8191
- recompute_index: int32 [32768], P('req'), may hold values from 0 to 1023, as said below
Outputs:
- mixed: bfloat16 [32768, 2048], P(('req', 'tp'))
Inputs may be any that keep to these rules, and one draw needn't show every extreme that they name: `request_lengths`: each request holds at least one group, they sum to 64, and some request holds exactly 3. `group_order`: every value appears once. `recompute_index`: the 512 positions of each group are distinct, increasing, and include 0 and 1023.
All inputs are finite; a program needn't handle non-finite values.
Results may differ from a plain program's by a relative error of at most 0.03.
Values may be sent and summed in bfloat16 or wider, within the bound.
No kernel may reach another device: no remote copies, remote signals or barrier semaphores. Data moves between devices by JAX's collectives and lax.ppermute only.
A program may use at most 128 MiB of HBM per device.

v0:
```python
import functools

import jax
import jax.numpy as jnp
from jax import lax
from jax.sharding import PartitionSpec as P
from jax.experimental import pallas as pl
from jax.experimental.pallas import tpu as pltpu

HEAD_DIM = 128
GROUP = 1024
MOST = 3


ROTARY_BASE = 10000.0
EPSILON = 1e-05
MASKED = -1e30


def from_behind(x, axis, by):
    length = lax.axis_size(axis)
    pairs = [(i, i + by) for i in range(length) if 0 <= i + by < length]
    return lax.ppermute(x, axis, pairs)


def frequencies(half_dim):
    indices = jnp.arange(half_dim, dtype=jnp.float32)
    return jnp.exp(indices * (-jnp.log(jnp.float32(ROTARY_BASE)) / half_dim))


def rotation_tables(angles, width):
    cosine = jnp.cos(angles)
    sine_part = jnp.sin(angles)
    repeats = width // (2 * angles.shape[-1])
    cos_full = jnp.tile(jnp.concatenate([cosine, cosine], axis=-1), (1, repeats))
    sin_full = jnp.tile(jnp.concatenate([-sine_part, sine_part], axis=-1), (1, repeats))
    return cos_full, sin_full


def rotate_flat(vectors, cos_full, sin_full):
    half_dim = HEAD_DIM // 2
    width = vectors.shape[-1]
    column = jnp.arange(width, dtype=jnp.int32) % HEAD_DIM
    partner = jnp.where(
        (column < half_dim)[None, :],
        jnp.roll(vectors, -half_dim, axis=1),
        jnp.roll(vectors, half_dim, axis=1),
    )
    return vectors * cos_full + partner * sin_full


def group_layout(request_lengths, group_order):
    group_count = group_order.shape[0]
    request_ends = jnp.cumsum(request_lengths)
    group_ids = jnp.arange(group_count, dtype=jnp.int32)
    group_request = jnp.sum((group_ids[:, None] >= request_ends[None, :]).astype(jnp.int32), axis=1)
    same_request = group_request[:, None] == group_request[None, :]
    earlier = group_order[None, :] < group_order[:, None]
    group_rank = jnp.sum((same_request & earlier).astype(jnp.int32), axis=1)
    return (group_request, group_rank)


def layer_norm(rows_in):
    values32 = rows_in.astype(jnp.float32)
    row_mean = jnp.mean(values32, axis=1, keepdims=True)
    centered = values32 - row_mean
    variance = jnp.mean(centered * centered, axis=1, keepdims=True)
    return (centered * lax.rsqrt(variance + EPSILON)).astype(jnp.bfloat16)


def own_attention_kernel(index_ref, query_ref, own_key_ref, own_value_ref, max_ref, sum_ref, acc_ref):
    scale = HEAD_DIM ** (-0.5)
    scores = (
        lax.dot_general(
            query_ref[...], own_key_ref[...], (((1,), (1,)), ((), ())),
            preferred_element_type=jnp.float32,
        )
        * scale
    )
    key_ids = lax.broadcasted_iota(jnp.int32, scores.shape, 1)
    visible = key_ids <= index_ref[...]
    scores = jnp.where(visible, scores, MASKED)
    row_max = jnp.max(scores, axis=1, keepdims=True)
    weights = jnp.where(visible, jnp.exp(scores - row_max), 0.0)
    max_ref[...] = jnp.broadcast_to(row_max, max_ref.shape)
    sum_ref[...] = jnp.broadcast_to(jnp.sum(weights, axis=1, keepdims=True), sum_ref.shape)
    acc_ref[...] = jnp.dot(
        weights.astype(jnp.bfloat16), own_value_ref[...], preferred_element_type=jnp.float32
    )


def far_attention_kernel(final, flags_ref, query_ref, max_ref, sum_ref, acc_ref, *refs):
    output_count = 1 if final else 3
    far_refs = refs[:-output_count]
    out_refs = refs[-output_count:]
    scale = HEAD_DIM ** (-0.5)
    query = query_ref[...]
    state = (max_ref[:, :1], sum_ref[:, :1], acc_ref[...])
    for slot in range(len(far_refs) // 2):
        key_ref, value_ref = far_refs[2 * slot : 2 * slot + 2]

        def block(carry, key_ref=key_ref, value_ref=value_ref):
            old_max, old_sum, old_acc = carry
            block_scores = (
                lax.dot_general(
                    query, key_ref[...], (((1,), (1,)), ((), ())),
                    preferred_element_type=jnp.float32,
                )
                * scale
            )
            new_max = jnp.maximum(old_max, jnp.max(block_scores, axis=1, keepdims=True))
            keep = jnp.exp(old_max - new_max)
            block_weights = jnp.exp(block_scores - new_max)
            return (
                new_max,
                keep * old_sum + jnp.sum(block_weights, axis=1, keepdims=True),
                keep * old_acc
                + jnp.dot(
                    block_weights.astype(jnp.bfloat16), value_ref[...],
                    preferred_element_type=jnp.float32,
                ),
            )

        state = lax.cond(flags_ref[slot] != 0, block, lambda carry: carry, state)
    if final:
        out_refs[0][...] = (state[2] / state[1]).astype(out_refs[0].dtype)
    else:
        out_refs[0][...] = jnp.broadcast_to(state[0], out_refs[0].shape)
        out_refs[1][...] = jnp.broadcast_to(state[1], out_refs[1].shape)
        out_refs[2][...] = state[2]


def fused_attention(flags, recompute_index, queries, joined_kv, far_parts):
    row_count, feature_width = queries.shape
    head_count = feature_width // HEAD_DIM
    key_count = joined_kv.shape[0]
    params = pltpu.CompilerParams(vmem_limit_bytes=48 * 1024 * 1024)
    head_block = pl.BlockSpec((row_count, HEAD_DIM), lambda h: (0, h))
    state_shape = jax.ShapeDtypeStruct((row_count, feature_width), jnp.float32)
    running = pl.pallas_call(
        own_attention_kernel,
        grid=(head_count,),
        in_specs=[
            pl.BlockSpec((row_count, 1), lambda h: (0, 0)),
            head_block,
            pl.BlockSpec((key_count, HEAD_DIM), lambda h: (0, h)),
            pl.BlockSpec((key_count, HEAD_DIM), lambda h: (0, h + head_count)),
        ],
        out_specs=[head_block, head_block, head_block],
        out_shape=[state_shape, state_shape, state_shape],
        compiler_params=params,
    )(recompute_index.reshape(row_count, 1), queries, joined_kv, joined_kv)

    def column_spec(rows, offset, slot=None):
        if slot is None:
            return pl.BlockSpec((rows, HEAD_DIM), lambda h, flags_ref: (0, h + offset))
        return pl.BlockSpec(
            (rows, HEAD_DIM), lambda h, flags_ref: (0, (h + offset) * flags_ref[slot])
        )

    for part_index, final in ((0, False), (1, True)):
        in_specs = [column_spec(row_count, 0)] * 4
        operands = [queries, *running]
        for slot, parts in enumerate(far_parts):
            part = parts[part_index]
            in_specs += [
                column_spec(part.shape[0], 0, slot),
                column_spec(part.shape[0], head_count, slot),
            ]
            operands += [part, part]
        out_spec = column_spec(row_count, 0)
        grid_spec = pltpu.PrefetchScalarGridSpec(
            num_scalar_prefetch=1,
            grid=(head_count,),
            in_specs=in_specs,
            out_specs=out_spec if final else [out_spec] * 3,
        )
        out_shape = (
            jax.ShapeDtypeStruct((row_count, feature_width), jnp.bfloat16)
            if final
            else [state_shape] * 3
        )
        running = pl.pallas_call(
            functools.partial(far_attention_kernel, final),
            grid_spec=grid_spec,
            out_shape=out_shape,
            compiler_params=params,
        )(flags, *operands)
    return running


def per_device(
    tokens,
    query_weight,
    kv_weight,
    out_weight,
    cached_keys,
    cached_values,
    request_lengths,
    group_order,
    group_offset,
    recompute_index,
):
    feature_width = query_weight.shape[1]
    half_dim = HEAD_DIM // 2
    group_count = group_order.shape[0]
    tp_size = lax.axis_size("tp")
    device = lax.axis_index("req")
    tp_index = lax.axis_index("tp")
    group_request, group_rank = group_layout(request_lengths, group_order)
    own_request = group_request[device]
    own_rank = group_rank[device]
    weight_pieces = [out_weight]
    for shift in range(1, tp_size):
        pairs = [(peer, (peer + shift) % tp_size) for peer in range(tp_size)]
        weight_pieces.append(lax.ppermute(out_weight, "tp", pairs))
    freq = frequencies(half_dim)
    key_count = cached_keys.shape[0]
    row_count = recompute_index.shape[0]

    rotation = (own_rank * GROUP - group_offset[device]).astype(jnp.float32)
    group_cos, group_sin = rotation_tables((rotation * freq)[None, :], feature_width)
    rotated_keys = rotate_flat(cached_keys.astype(jnp.float32), group_cos, group_sin).astype(
        jnp.bfloat16
    )
    cached_kv = jnp.concatenate([rotated_keys, cached_values], axis=1)

    key_ids = jnp.arange(key_count, dtype=jnp.int32)
    placement = key_ids[:, None] == recompute_index[None, :]
    replaced = jnp.any(placement, axis=1)
    replaced_before = jnp.sum((recompute_index[None, :] < key_ids[:, None]).astype(jnp.int32), axis=1)
    kept_slot = key_ids - replaced_before
    packing = (~replaced)[None, :] & (
        jnp.arange(key_count - row_count, dtype=jnp.int32)[:, None] == kept_slot[None, :]
    )
    kept_kv = jnp.dot(
        packing.astype(jnp.bfloat16), cached_kv, preferred_element_type=jnp.float32
    ).astype(jnp.bfloat16)

    distances = [distance for distance in range(1, MOST)] + [
        -distance for distance in range(1, MOST)
    ]
    far_kept = [from_behind(kept_kv, "req", distance) for distance in distances]

    local_rows = layer_norm(tokens)
    row_pieces = [local_rows]
    for shift in range(1, tp_size):
        pairs = [(peer, (peer + shift) % tp_size) for peer in range(tp_size)]
        row_pieces.append(lax.ppermute(local_rows, "tp", pairs))
    row_stack = jnp.stack(row_pieces)
    normalized = jnp.concatenate(
        [row_stack[(tp_index - peer) % tp_size] for peer in range(tp_size)], axis=0
    )
    query_part = jnp.dot(normalized, query_weight, preferred_element_type=jnp.float32)
    kv_part = jnp.einsum("nd,dkc->knc", normalized, kv_weight, preferred_element_type=jnp.float32)
    key_part = kv_part[0]
    value_part = kv_part[1]
    positions = (own_rank * GROUP + recompute_index).astype(jnp.float32)
    row_cos, row_sin = rotation_tables(positions[:, None] * freq[None, :], feature_width)
    queries = rotate_flat(query_part, row_cos, row_sin).astype(jnp.bfloat16)
    fresh_keys = rotate_flat(key_part, row_cos, row_sin).astype(jnp.bfloat16)
    fresh_values = value_part.astype(jnp.bfloat16)
    fresh_kv = jnp.concatenate([fresh_keys, fresh_values], axis=1)
    far_fresh = [from_behind(fresh_kv, "req", distance) for distance in distances]

    placed_kv = jnp.dot(
        placement.astype(jnp.bfloat16), fresh_kv, preferred_element_type=jnp.float32
    ).astype(jnp.bfloat16)
    joined_kv = jnp.where(replaced[:, None], placed_kv, cached_kv)
    flags = []
    for distance in distances:
        source_index = jnp.clip(device - distance, 0, group_count - 1)
        source_inside = (device - distance >= 0) & (device - distance < group_count)
        needed = (
            source_inside
            & (group_request[source_index] == own_request)
            & (group_rank[source_index] < own_rank)
        )
        flags.append(needed.astype(jnp.int32))
    attention = fused_attention(
        jnp.stack(flags), recompute_index, queries, joined_kv, list(zip(far_kept, far_fresh))
    )

    chunk = row_count // tp_size

    def rows_for(peer):
        return lax.dynamic_slice_in_dim(attention, peer * chunk, chunk, 0)

    pieces = [rows_for(tp_index)]
    for shift in range(1, tp_size):
        pairs = [(peer, (peer + shift) % tp_size) for peer in range(tp_size)]
        pieces.append(lax.ppermute(rows_for((tp_index + shift) % tp_size), "tp", pairs))
    mixed = jnp.dot(
        jnp.concatenate(pieces, axis=1),
        jnp.concatenate(weight_pieces, axis=0),
        preferred_element_type=jnp.float32,
    )
    return mixed.astype(jnp.bfloat16)


def solution(mesh):
    placed = (
        P(("req", "tp"), None),
        P(None, "tp"),
        P(None, None, "tp"),
        P("tp", None),
        P("req", "tp"),
        P("req", "tp"),
        P(),
        P(),
        P(),
        P("req"),
    )

    return jax.shard_map(
        per_device, mesh=mesh, in_specs=placed, out_specs=P(("req", "tp"), None), check_vma=False
    )
```

profile of v0, /device:TPU:56, one launch (start us, length us, event | category | flops | bytes accessed | tf_op | source)
XLA Modules:
  0.0 174.1 jit_solution(6388757347853313133)
XLA Ops:
  0.0 1.3 convert_reduce_fusion.1
  1.4 1.3 fusion.32
  2.7 2.2 %fusion.33 = bf16[128,2048]{1,0:T(8,128)(2,1)} fusion(bf16[128,2048]{1,0:T(8,128)(2,1)} %param.10, f32[128]{0:T(128)S(1)} %add_rsqrt_fusion, f32[128]{0:T(128)S(1)} %broadcast_multiply_fusion), kind=kLoop, calls=%fused_computation.35 | loop fusion | flops 1048576 | bytes 1049600 | tf_op jit(solution)/shard_map/convert_element_type | solution.py:68
  4.9 1.5 collective-permute-start
  6.4 2.7 %collective-permute-start.1 = (bf16[128,2048]{1,0:T(8,128)(2,1)}, bf16[128,2048]{1,0:T(8,128)(2,1)}, u32[]{:S(2)}, u32[]{:S(2)}) collective-permute-start(bf16[128,2048]{1,0:T(8,128)(2,1)} %fusion.33), channel_id=1, source_target_pairs={{0,2},{1,3},{2,0},{3,1},{4,6},{5,7},{6,4},{7,5},{8,10},{9,11},{10,... | collective-permute-start | bytes 1572872 | tf_op jit(solution)/shard_map/ppermute | solution.py:249
  9.1 1.4 collective-permute-start.2
  16.7 2.2 %fusion.27 = bf16[512,1024]{1,0:T(8,128)(2,1)} fusion(bf16[1024,512]{1,0:T(8,128)(2,1)S(1)} %copy-done.16, bf16[1024,512]{1,0:T(8,128)(2,1)S(1)} %fusion.15, s32[1024]{0:T(1024)S(1)} %iota_subtract_fusion, pred[1024]{0:T(1024)(128)(4,1)S(1)} %not.7), kind=kOutput, calls=%fused_computation.29 | convolution fusion | flops 1079508992 | bytes 3150848 | tf_op jit(solution)/shard_map/dot_general | solution.py:236
  18.9 2.0 %collective-permute-start.3 = (bf16[512,1024]{1,0:T(8,128)(2,1)}, bf16[512,1024]{1,0:T(8,128)(2,1)}, u32[]{:S(2)}, u32[]{:S(2)}) collective-permute-start(bf16[512,1024]{1,0:T(8,128)(2,1)} %fusion.27), channel_id=1, source_target_pairs={{0,4},{4,8},{8,12},{12,16},{16,20},{20,24},{24,28},{28,32},{32,36}... | collective-permute-start | bytes 3145736 | tf_op jit(solution)/shard_map/ppermute | solution.py:23
  21.0 3.5 %collective-permute-start.4 = (bf16[512,1024]{1,0:T(8,128)(2,1)}, bf16[512,1024]{1,0:T(8,128)(2,1)}, u32[]{:S(2)}, u32[]{:S(2)}) collective-permute-start(bf16[512,1024]{1,0:T(8,128)(2,1)} %fusion.27), channel_id=1, source_target_pairs={{0,8},{4,12},{8,16},{12,20},{16,24},{20,28},{24,32},{28,36},{32,40... | collective-permute-start | bytes 3145736 | tf_op jit(solution)/shard_map/ppermute | solution.py:23
  26.9 3.4 %collective-permute-start.5 = (bf16[512,1024]{1,0:T(8,128)(2,1)}, bf16[512,1024]{1,0:T(8,128)(2,1)S(1)}, u32[]{:S(2)}, u32[]{:S(2)}) collective-permute-start(bf16[512,1024]{1,0:T(8,128)(2,1)} %fusion.27), channel_id=1, source_target_pairs={{4,0},{8,4},{12,8},{16,12},{20,16},{24,20},{28,24},{32,28},{36,32}... | collective-permute-start | bytes 3145736 | tf_op jit(solution)/shard_map/ppermute | solution.py:23
  30.3 2.0 %collective-permute-done.1 = bf16[128,2048]{1,0:T(8,128)(2,1)} collective-permute-done((bf16[128,2048]{1,0:T(8,128)(2,1)}, bf16[128,2048]{1,0:T(8,128)(2,1)}, u32[]{:S(2)}, u32[]{:S(2)}) %collective-permute-start.1) | collective-permute-done | bytes 524320 | tf_op jit(solution)/shard_map/ppermute | solution.py:249
  32.3 2.8 %collective-permute-start.6 = (bf16[512,1024]{1,0:T(8,128)(2,1)}, bf16[512,1024]{1,0:T(8,128)(2,1)S(1)}, u32[]{:S(2)}, u32[]{:S(2)}) collective-permute-start(bf16[512,1024]{1,0:T(8,128)(2,1)} %fusion.27), channel_id=1, source_target_pairs={{8,0},{12,4},{16,8},{20,12},{24,16},{28,20},{32,24},{36,28},{40,32... | collective-permute-start | bytes 3145736 | tf_op jit(solution)/shard_map/ppermute | solution.py:23
  35.1 1.6 pad_maximum_fusion
  36.9 1.2 fusion.49
  39.1 2.3 %fusion.22 = f32[2,512,512]{2,1,0:T(8,128)S(1)} fusion(bf16[2048,2,512]{2,1,0:T(2,128)(2,1)S(1)} %copy-done.15, bf16[128,2048]{1,0:T(8,128)(2,1)S(1)} %get-tuple-element.20, bf16[128,2048]{1,0:T(8,128)(2,1)S(1)} %get-tuple-element.21, bf16[128,2048]{1,0:T(8,128)(2,1)S(1)} %get-tuple-element.22, bf16[128,2048]{1,0:T(8,128)(2,1)S(1)} %get-tuple-element.19), kind=kOutput, calls=%fused_computation.28 | convolution fusion | flops 2155872256 | bytes 8388608 | tf_op jit(solution)/shard_map/nd,dkc->knc/dot_general | solution.py:255
  43.4 1.2 fusion.37
  44.6 1.2 pad_maximum_fusion.4
  45.7 2.3 %collective-permute-start.10 = (bf16[512,1024]{1,0:T(8,128)(2,1)}, bf16[512,1024]{1,0:T(8,128)(2,1)S(1)}, u32[]{:S(2)}, u32[]{:S(2)}) collective-permute-start(bf16[512,1024]{1,0:T(8,128)(2,1)} %pad_maximum_fusion.4), channel_id=1, source_target_pairs={{8,0},{12,4},{16,8},{20,12},{24,16},{28,20},{32,24},{36,28},{40,32... | collective-permute-start | bytes 3145736 | tf_op jit(solution)/shard_map/ppermute | solution.py:23
  48.1 1.9 %collective-permute-start.7 = (bf16[512,1024]{1,0:T(8,128)(2,1)}, bf16[512,1024]{1,0:T(8,128)(2,1)S(1)}, u32[]{:S(2)}, u32[]{:S(2)}) collective-permute-start(bf16[512,1024]{1,0:T(8,128)(2,1)} %pad_maximum_fusion.4), channel_id=1, source_target_pairs={{0,4},{4,8},{8,12},{12,16},{16,20},{20,24},{24,28},{28,32},{32,36}... | collective-permute-start | bytes 3145736 | tf_op jit(solution)/shard_map/ppermute | solution.py:23
  50.1 1.3 collective-permute-done.5.refs_4_.refs_5_
  51.7 26.6 %collective-permute-done.6.refs_6_.refs_7_ = bf16[512,1024]{1,0:T(8,128)(2,1)S(1)} collective-permute-done((bf16[512,1024]{1,0:T(8,128)(2,1)}, bf16[512,1024]{1,0:T(8,128)(2,1)S(1)}, u32[]{:S(2)}, u32[]{:S(2)}) %collective-permute-start.6) | collective-permute-done | bytes 1048608 | tf_op jit(solution)/shard_map/ppermute | solution.py:23
  78.3 1.0 collective-permute-start.16
  79.3 12.6 %collective-permute-done.10.refs_6_.refs_7_ = bf16[512,1024]{1,0:T(8,128)(2,1)S(1)} collective-permute-done((bf16[512,1024]{1,0:T(8,128)(2,1)}, bf16[512,1024]{1,0:T(8,128)(2,1)S(1)}, u32[]{:S(2)}, u32[]{:S(2)}) %collective-permute-start.10) | collective-permute-done | bytes 1048608 | tf_op jit(solution)/shard_map/ppermute | solution.py:23
  91.9 1.9 %collective-permute-start.8 = (bf16[512,1024]{1,0:T(8,128)(2,1)}, bf16[512,1024]{1,0:T(8,128)(2,1)}, u32[]{:S(2)}, u32[]{:S(2)}) collective-permute-start(bf16[512,1024]{1,0:T(8,128)(2,1)} %pad_maximum_fusion.4), channel_id=1, source_target_pairs={{0,8},{4,12},{8,16},{12,20},{16,24},{20,28},{24,32},{28,36},{32,40... | collective-permute-start | bytes 3145736 | tf_op jit(solution)/shard_map/ppermute | solution.py:23
  94.8 2.1 %collective-permute-start.9 = (bf16[512,1024]{1,0:T(8,128)(2,1)}, bf16[512,1024]{1,0:T(8,128)(2,1)}, u32[]{:S(2)}, u32[]{:S(2)}) collective-permute-start(bf16[512,1024]{1,0:T(8,128)(2,1)} %pad_maximum_fusion.4), channel_id=1, source_target_pairs={{4,0},{8,4},{12,8},{16,12},{20,16},{24,20},{28,24},{32,28},{36,32}... | collective-permute-start | bytes 3145736 | tf_op jit(solution)/shard_map/ppermute | solution.py:23
  107.3 2.8 %convert_select_fusion.own_key_ref.own_value_ref = bf16[1024,1024]{1,0:T(8,128)(2,1)S(1)} fusion(pred[1024]{0:T(1024)(128)(4,1)S(1)} %fusion.18, bf16[1024,512]{1,0:T(8,128)(2,1)} %param.15, bf16[1024,512]{1,0:T(8,128)(2,1)} %copy-done.10, s32[512]{0:T(512)S(1)} %copy-done.12, bf16[512,512]{1,0:T(8,128)(2,1)S(1)} %fusion.41, bf16[512,512]{1,0:T(8,128)(2,1)} %copy-done.9), kind=kOutput, calls=%fused_computation.22 | convolution fusion | flops 1082654720 | bytes 5245952 | tf_op jit(solution)/shard_map/dot_general | solution.py:266
  110.2 8.4 %shard_map.100 = (f32[512,512]{1,0:T(8,128)S(1)}, f32[512,512]{1,0:T(8,128)S(1)}, f32[512,512]{1,0:T(8,128)S(1)}) custom-call(s32[512,1]{1,0:T(8,128)S(1)} %copy.36.index_ref, bf16[512,512]{1,0:T(8,128)(2,1)S(1)} %get-tuple-element.18.query_ref, bf16[1024,1024]{1,0:T(8,128)(2,1)S(1)} %convert_select_fusion.own_key_ref.own_value_ref, ...), custom_call_target="tpu_custom_call" | custom-call | tf_op jit(solution)/shard_map/pallas_call | solution.py:140
  119.5 17.6 %shard_map.101 = (f32[512,512]{1,0:T(8,128)S(1)}, f32[512,512]{1,0:T(8,128)S(1)}, f32[512,512]{1,0:T(8,128)S(1)}) custom-call(s32[4]{0:T(128)S(1)} %add_convert_fusion.1.flags_ref, bf16[512,512]{1,0:T(8,128)(2,1)S(1)} %get-tuple-element.18.query_ref, f32[512,512]{1,0:T(8,128)S(1)} %get-tuple-element.11.max_ref, f32[512,512]{1,0:T(8,128)S(1)} %get-tuple-element.12.sum_ref, ...), custom_call_target="tpu_custom_call" | custom-call | tf_op jit(solution)/shard_map/pallas_call | solution.py:183
  137.2 17.1 %shard_map.102 = bf16[512,512]{1,0:T(8,128)(2,1)S(1)} custom-call(s32[4]{0:T(128)S(1)} %add_convert_fusion.1.flags_ref, bf16[512,512]{1,0:T(8,128)(2,1)S(1)} %get-tuple-element.18.query_ref, f32[512,512]{1,0:T(8,128)S(1)} %get-tuple-element.14.max_ref, f32[512,512]{1,0:T(8,128)S(1)} %get-tuple-element.15.sum_ref, f32[512,512]{1,0:T(8,128)S(1)} %get-tuple-element.16.acc_ref, ...), custom_call_target="tpu_custom_call" | custom-call | tf_op jit(solution)/shard_map/pallas_call | solution.py:183
  155.9 8.4 %collective-permute-done.11 = bf16[128,512]{1,0:T(8,128)(2,1)S(1)} collective-permute-done((bf16[128,512]{1,0:T(8,128)(2,1)S(1)}, bf16[128,512]{1,0:T(8,128)(2,1)S(1)}, u32[]{:S(2)}, u32[]{:S(2)}) %collective-permute-start.11) | collective-permute-done | bytes 131104 | tf_op jit(solution)/shard_map/ppermute | solution.py:292
  164.3 5.0 %collective-permute-done.13 = bf16[128,512]{1,0:T(8,128)(2,1)S(1)} collective-permute-done((bf16[128,512]{1,0:T(8,128)(2,1)S(1)}, bf16[128,512]{1,0:T(8,128)(2,1)S(1)}, u32[]{:S(2)}, u32[]{:S(2)}) %collective-permute-start.13) | collective-permute-done | bytes 131104 | tf_op jit(solution)/shard_map/ppermute | solution.py:292
  169.2 4.9 %fusion.10 = bf16[128,2048]{1,0:T(8,128)(2,1)} fusion(bf16[512,2048]{1,0:T(8,128)(2,1)} %collective-permute-done.16, bf16[512,2048]{1,0:T(8,128)(2,1)} %collective-permute-done.15, bf16[512,2048]{1,0:T(8,128)(2,1)} %collective-permute-done.14, bf16[512,2048]{1,0:T(8,128)(2,1)} %param.13, bf16[128,512]{1,0:T(8,128)(2,1)S(1)} %collective-permute-done.13, ...), kind=kOutput, calls=%fused_computation.10 | convolution fusion | flops 1109655552 | bytes 9437184 | tf_op jit(solution)/shard_map/dot_general | solution.py:293
  (92 shorter events, 14.2 us)
Async XLA Ops:
  0.0 36.9 %copy-start = (bf16[2048,512]{1,0:T(8,128)(2,1)S(1)}, bf16[2048,512]{1,0:T(8,128)(2,1)}, u32[]{:S(2)}) copy-start(bf16[2048,512]{1,0:T(8,128)(2,1)} %param.11) | copy-start | bytes 6291460
  0.0 10.5 %copy-start.14 = (s32[32]{0:T(128)S(1)}, s32[32]{0:T(128)}, u32[]{:S(2)}) copy-start(s32[32]{0:T(128)} %param.16) | copy-start | bytes 388
  0.0 10.9 %copy-start.13 = (s32[64]{0:T(128)S(1)}, s32[64]{0:T(128)}, u32[]{:S(2)}) copy-start(s32[64]{0:T(128)} %param.17) | copy-start | bytes 772
  0.0 11.1 %copy-start.17 = (s32[64]{0:T(128)S(1)}, s32[64]{0:T(128)}, u32[]{:S(2)}) copy-start(s32[64]{0:T(128)} %param.18) | copy-start | bytes 772
  0.0 13.9 %copy-start.4 = (bf16[1024,512]{1,0:T(8,128)(2,1)S(1)}, bf16[1024,512]{1,0:T(8,128)(2,1)}, u32[]{:S(2)}) copy-start(bf16[1024,512]{1,0:T(8,128)(2,1)} %param.14) | copy-start | bytes 3145732
  4.9 22.0 %collective-permute-start = (bf16[128,2048]{1,0:T(8,128)(2,1)}, bf16[128,2048]{1,0:T(8,128)(2,1)}, u32[]{:S(2)}, u32[]{:S(2)}) collective-permute-start(bf16[128,2048]{1,0:T(8,128)(2,1)} %fusion.33), channel_id=1, source_target_pairs={{0,1},{1,2},{2,3},{3,0},{4,5},{5,6},{6,7},{7,4},{8,9},{9,10},{10,1... | collective-permute-start | bytes 1572872 | tf_op jit(solution)/shard_map/ppermute | solution.py:249
  6.4 25.9 %collective-permute-start.1 = (bf16[128,2048]{1,0:T(8,128)(2,1)}, bf16[128,2048]{1,0:T(8,128)(2,1)}, u32[]{:S(2)}, u32[]{:S(2)}) collective-permute-start(bf16[128,2048]{1,0:T(8,128)(2,1)} %fusion.33), channel_id=1, source_target_pairs={{0,2},{1,3},{2,0},{3,1},{4,6},{5,7},{6,4},{7,5},{8,10},{9,11},{10,... | collective-permute-start | bytes 1572872 | tf_op jit(solution)/shard_map/ppermute | solution.py:249
  9.1 26.0 %collective-permute-start.2 = (bf16[128,2048]{1,0:T(8,128)(2,1)}, bf16[128,2048]{1,0:T(8,128)(2,1)}, u32[]{:S(2)}, u32[]{:S(2)}) collective-permute-start(bf16[128,2048]{1,0:T(8,128)(2,1)} %fusion.33), channel_id=1, source_target_pairs={{0,3},{1,0},{2,1},{3,2},{4,7},{5,4},{6,5},{7,6},{8,11},{9,8},{10,9... | collective-permute-start | bytes 1572872 | tf_op jit(solution)/shard_map/ppermute | solution.py:249
  15.5 1.2 copy-start.16
  16.7 2.2 %copy-start.10 = (bf16[1024,512]{1,0:T(8,128)(2,1)}, bf16[1024,512]{1,0:T(8,128)(2,1)S(1)}, u32[]{:S(2)}) copy-start(bf16[1024,512]{1,0:T(8,128)(2,1)S(1)} %fusion.15) | copy-start | bytes 3145732
  18.9 7.6 %copy-start.5 = (bf16[128,2048]{1,0:T(8,128)(2,1)S(1)}, bf16[128,2048]{1,0:T(8,128)(2,1)}, u32[]{:S(2)}) copy-start(bf16[128,2048]{1,0:T(8,128)(2,1)} %param.10) | copy-start | bytes 1572868
  18.9 29.1 %collective-permute-start.3 = (bf16[512,1024]{1,0:T(8,128)(2,1)}, bf16[512,1024]{1,0:T(8,128)(2,1)}, u32[]{:S(2)}, u32[]{:S(2)}) collective-permute-start(bf16[512,1024]{1,0:T(8,128)(2,1)} %fusion.27), channel_id=1, source_target_pairs={{0,4},{4,8},{8,12},{12,16},{16,20},{20,24},{24,28},{28,32},{32,36}... | collective-permute-start | bytes 3145736 | tf_op jit(solution)/shard_map/ppermute | solution.py:23
  21.0 29.0 %collective-permute-start.4 = (bf16[512,1024]{1,0:T(8,128)(2,1)}, bf16[512,1024]{1,0:T(8,128)(2,1)}, u32[]{:S(2)}, u32[]{:S(2)}) collective-permute-start(bf16[512,1024]{1,0:T(8,128)(2,1)} %fusion.27), channel_id=1, source_target_pairs={{0,8},{4,12},{8,16},{12,20},{16,24},{20,28},{24,32},{28,36},{32,40... | collective-permute-start | bytes 3145736 | tf_op jit(solution)/shard_map/ppermute | solution.py:23
  26.9 24.5 %collective-permute-start.5 = (bf16[512,1024]{1,0:T(8,128)(2,1)}, bf16[512,1024]{1,0:T(8,128)(2,1)S(1)}, u32[]{:S(2)}, u32[]{:S(2)}) collective-permute-start(bf16[512,1024]{1,0:T(8,128)(2,1)} %fusion.27), channel_id=1, source_target_pairs={{4,0},{8,4},{12,8},{16,12},{20,16},{24,20},{28,24},{32,28},{36,32}... | collective-permute-start | bytes 3145736 | tf_op jit(solution)/shard_map/ppermute | solution.py:23
  32.3 46.0 %collective-permute-start.6 = (bf16[512,1024]{1,0:T(8,128)(2,1)}, bf16[512,1024]{1,0:T(8,128)(2,1)S(1)}, u32[]{:S(2)}, u32[]{:S(2)}) collective-permute-start(bf16[512,1024]{1,0:T(8,128)(2,1)} %fusion.27), channel_id=1, source_target_pairs={{8,0},{12,4},{16,8},{20,12},{24,16},{28,20},{32,24},{36,28},{40,32... | collective-permute-start | bytes 3145736 | tf_op jit(solution)/shard_map/ppermute | solution.py:23
  36.9 2.2 %copy-start.15 = (bf16[2048,2,512]{2,1,0:T(2,128)(2,1)S(1)}, bf16[2048,2,512]{2,1,0:T(2,128)(2,1)}, u32[]{:S(2)}) copy-start(bf16[2048,2,512]{2,1,0:T(2,128)(2,1)} %param.12) | copy-start | bytes 12582916
  44.6 49.3 %copy-start.9 = (bf16[512,512]{1,0:T(8,128)(2,1)}, bf16[512,512]{1,0:T(8,128)(2,1)S(1)}, u32[]{:S(2)}) copy-start(bf16[512,512]{1,0:T(8,128)(2,1)S(1)} %get-tuple-element.17) | copy-start | bytes 1572868
  45.7 46.2 %collective-permute-start.10 = (bf16[512,1024]{1,0:T(8,128)(2,1)}, bf16[512,1024]{1,0:T(8,128)(2,1)S(1)}, u32[]{:S(2)}, u32[]{:S(2)}) collective-permute-start(bf16[512,1024]{1,0:T(8,128)(2,1)} %pad_maximum_fusion.4), channel_id=1, source_target_pairs={{8,0},{12,4},{16,8},{20,12},{24,16},{28,20},{32,24},{36,28},{40,32... | collective-permute-start | bytes 3145736 | tf_op jit(solution)/shard_map/ppermute | solution.py:23
  48.1 45.7 %collective-permute-start.7 = (bf16[512,1024]{1,0:T(8,128)(2,1)}, bf16[512,1024]{1,0:T(8,128)(2,1)S(1)}, u32[]{:S(2)}, u32[]{:S(2)}) collective-permute-start(bf16[512,1024]{1,0:T(8,128)(2,1)} %pad_maximum_fusion.4), channel_id=1, source_target_pairs={{0,4},{4,8},{8,12},{12,16},{16,20},{20,24},{24,28},{28,32},{32,36}... | collective-permute-start | bytes 3145736 | tf_op jit(solution)/shard_map/ppermute | solution.py:23
  50.0 119.2 %collective-permute-start.14 = (bf16[512,2048]{1,0:T(8,128)(2,1)}, bf16[512,2048]{1,0:T(8,128)(2,1)}, u32[]{:S(2)}, u32[]{:S(2)}) collective-permute-start(bf16[512,2048]{1,0:T(8,128)(2,1)} %param.13), channel_id=1, source_target_pairs={{0,1},{1,2},{2,3},{3,0},{4,5},{5,6},{6,7},{7,4},{8,9},{9,10},{10,1... | collective-permute-start | bytes 6291464 | tf_op jit(solution)/shard_map/ppermute | solution.py:216
  51.5 42.4 %copy-start.6 = (bf16[512,1024]{1,0:T(8,128)(2,1)}, bf16[512,1024]{1,0:T(8,128)(2,1)S(1)}, u32[]{:S(2)}) copy-start(bf16[512,1024]{1,0:T(8,128)(2,1)S(1)} %collective-permute-done.5.refs_4_.refs_5_) | copy-start | bytes 3145732
  51.5 117.8 %collective-permute-start.15 = (bf16[512,2048]{1,0:T(8,128)(2,1)}, bf16[512,2048]{1,0:T(8,128)(2,1)}, u32[]{:S(2)}, u32[]{:S(2)}) collective-permute-start(bf16[512,2048]{1,0:T(8,128)(2,1)} %param.13), channel_id=1, source_target_pairs={{0,2},{1,3},{2,0},{3,1},{4,6},{5,7},{6,4},{7,5},{8,10},{9,11},{10,... | collective-permute-start | bytes 6291464 | tf_op jit(solution)/shard_map/ppermute | solution.py:216
  78.3 15.6 %copy-start.7 = (bf16[512,1024]{1,0:T(8,128)(2,1)}, bf16[512,1024]{1,0:T(8,128)(2,1)S(1)}, u32[]{:S(2)}) copy-start(bf16[512,1024]{1,0:T(8,128)(2,1)S(1)} %collective-permute-done.6.refs_6_.refs_7_) | copy-start | bytes 3145732
  78.3 91.0 %collective-permute-start.16 = (bf16[512,2048]{1,0:T(8,128)(2,1)}, bf16[512,2048]{1,0:T(8,128)(2,1)}, u32[]{:S(2)}, u32[]{:S(2)}) collective-permute-start(bf16[512,2048]{1,0:T(8,128)(2,1)} %param.13), channel_id=1, source_target_pairs={{0,3},{1,0},{2,1},{3,2},{4,7},{5,4},{6,5},{7,6},{8,11},{9,8},{10,9... | collective-permute-start | bytes 6291464 | tf_op jit(solution)/shard_map/ppermute | solution.py:216
  91.9 2.0 %copy-start.8 = (bf16[512,1024]{1,0:T(8,128)(2,1)}, bf16[512,1024]{1,0:T(8,128)(2,1)S(1)}, u32[]{:S(2)}) copy-start(bf16[512,1024]{1,0:T(8,128)(2,1)S(1)} %collective-permute-done.10.refs_6_.refs_7_) | copy-start | bytes 3145732
  91.9 45.3 %collective-permute-start.8 = (bf16[512,1024]{1,0:T(8,128)(2,1)}, bf16[512,1024]{1,0:T(8,128)(2,1)}, u32[]{:S(2)}, u32[]{:S(2)}) collective-permute-start(bf16[512,1024]{1,0:T(8,128)(2,1)} %pad_maximum_fusion.4), channel_id=1, source_target_pairs={{0,8},{4,12},{8,16},{12,20},{16,24},{20,28},{24,32},{28,36},{32,40... | collective-permute-start | bytes 3145736 | tf_op jit(solution)/shard_map/ppermute | solution.py:23
  94.8 42.3 %collective-permute-start.9 = (bf16[512,1024]{1,0:T(8,128)(2,1)}, bf16[512,1024]{1,0:T(8,128)(2,1)}, u32[]{:S(2)}, u32[]{:S(2)}) collective-permute-start(bf16[512,1024]{1,0:T(8,128)(2,1)} %pad_maximum_fusion.4), channel_id=1, source_target_pairs={{4,0},{8,4},{12,8},{16,12},{20,16},{24,20},{28,24},{32,28},{36,32}... | collective-permute-start | bytes 3145736 | tf_op jit(solution)/shard_map/ppermute | solution.py:23
  118.5 1.0 copy-start.3
  119.5 17.7 %copy-start.2 = (bf16[512,1024]{1,0:T(8,128)(2,1)S(1)}, bf16[512,1024]{1,0:T(8,128)(2,1)}, u32[]{:S(2)}) copy-start(bf16[512,1024]{1,0:T(8,128)(2,1)} %copy-done.1) | copy-start | bytes 3145732
  154.3 9.9 %collective-permute-start.11 = (bf16[128,512]{1,0:T(8,128)(2,1)S(1)}, bf16[128,512]{1,0:T(8,128)(2,1)S(1)}, u32[]{:S(2)}, u32[]{:S(2)}) collective-permute-start(bf16[128,512]{1,0:T(8,128)(2,1)S(1)} %get-tuple-element.38), channel_id=1, source_target_pairs={{0,1},{1,2},{2,3},{3,0},{4,5},{5,6},{6,7},{7,4},{8,9},{9,10},{10,1... | collective-permute-start | bytes 393224 | tf_op jit(solution)/shard_map/ppermute | solution.py:292
  155.0 9.2 %collective-permute-start.12 = (bf16[128,512]{1,0:T(8,128)(2,1)S(1)}, bf16[128,512]{1,0:T(8,128)(2,1)S(1)}, u32[]{:S(2)}, u32[]{:S(2)}) collective-permute-start(bf16[128,512]{1,0:T(8,128)(2,1)S(1)} %get-tuple-element.37), channel_id=1, source_target_pairs={{0,2},{1,3},{2,0},{3,1},{4,6},{5,7},{6,4},{7,5},{8,10},{9,11},{10,... | collective-permute-start | bytes 393224 | tf_op jit(solution)/shard_map/ppermute | solution.py:292
  164.3 5.0 %collective-permute-start.13 = (bf16[128,512]{1,0:T(8,128)(2,1)S(1)}, bf16[128,512]{1,0:T(8,128)(2,1)S(1)}, u32[]{:S(2)}, u32[]{:S(2)}) collective-permute-start(bf16[128,512]{1,0:T(8,128)(2,1)S(1)} %get-tuple-element.36), channel_id=1, source_target_pairs={{0,3},{1,0},{2,1},{3,2},{4,7},{5,4},{6,5},{7,6},{8,11},{9,8},{10,9... | collective-permute-start | bytes 393224 | tf_op jit(solution)/shard_map/ppermute | solution.py:292
  (3 other events, 2.7 us)
where the time goes:
time: 175 us; the launch traced here: 174 us
  waiting for transfers between devices  55.9 us (32%)
  Pallas kernels  43.1 us (25%)
  starting transfers between devices  28.5 us (16%)
  matrix products  13.5 us (8%)
  other arithmetic  13.3 us (8%)
  between operations  12 us (7%)
  local copies, waits for them, and re-layouts  7.75 us (4%)
    ppermute x8, waiting for transfers between devices, from_behind(): return lax.ppermute(x, axis, pairs)  40.5 us
    pallas_call x2, Pallas kernels, fused_attention(): pl.pallas_call(functools.partial(far_attention_kernel, final), grid_spec=...  34.7 us
    ppermute x8, starting transfers between devices, from_behind(): return lax.ppermute(x, axis, pairs)  20 us
    ppermute x3, waiting for transfers between devices, per_device(): lax.ppermute(rows_for((tp_index + shift) % tp_size), 'tp', pairs)  13.3 us
    pallas_call x1, Pallas kernels, fused_attention(): pl.pallas_call(own_attention_kernel, grid=(head_count,), in_specs=[pl.Blo...  8.38 us
    ppermute x3, starting transfers between devices, per_device(): row_pieces.append(lax.ppermute(local_rows, 'tp', pairs))  5.65 us
    dot_general x1, matrix products, per_device(): jnp.dot(jnp.concatenate(pieces, axis=1), jnp.concatenate(weight_pieces, a...  4.86 us
    unnamed x36, local copies, waits for them, and re-layouts  3.79 us
  transfers between devices with their start and end apart: 17, of which 6 were waited for; matrix products, arithmetic and copies ran while one was open for 12% of the time, Pallas kernels for 25%

commit v1 on v0

--- a/solution.py
+++ b/solution.py
@@ -81,7 +81,7 @@
     visible = key_ids <= index_ref[...]
     scores = jnp.where(visible, scores, MASKED)
     row_max = jnp.max(scores, axis=1, keepdims=True)
-    weights = jnp.where(visible, jnp.exp(scores - row_max), 0.0)
+    weights = jnp.exp(scores - row_max)
     max_ref[...] = jnp.broadcast_to(row_max, max_ref.shape)
     sum_ref[...] = jnp.broadcast_to(jnp.sum(weights, axis=1, keepdims=True), sum_ref.shape)
     acc_ref[...] = jnp.dot(
@@ -286,15 +286,11 @@
     def rows_for(peer):
         return lax.dynamic_slice_in_dim(attention, peer * chunk, chunk, 0)
 
-    pieces = [rows_for(tp_index)]
+    mixed = jnp.dot(rows_for(tp_index), weight_pieces[0], preferred_element_type=jnp.float32)
     for shift in range(1, tp_size):
         pairs = [(peer, (peer + shift) % tp_size) for peer in range(tp_size)]
-        pieces.append(lax.ppermute(rows_for((tp_index + shift) % tp_size), "tp", pairs))
-    mixed = jnp.dot(
-        jnp.concatenate(pieces, axis=1),
-        jnp.concatenate(weight_pieces, axis=0),
-        preferred_element_type=jnp.float32,
-    )
+        arrived = lax.ppermute(rows_for((tp_index + shift) % tp_size), "tp", pairs)
+        mixed = mixed + jnp.dot(arrived, weight_pieces[shift], preferred_element_type=jnp.float32)
     return mixed.astype(jnp.bfloat16)
 
 

time: 175 us -> 174 us (level)
  the two profiles are of different devices: /device:TPU:56 before, /device:TPU:1 now
where the time goes in v1:
time: 174 us; the launch traced here: 170 us
  starting transfers between devices  44.2 us (25%)
  Pallas kernels  42.1 us (24%)
  waiting for transfers between devices  33.3 us (19%)
  matrix products  18 us (10%)
  other arithmetic  13.5 us (8%)
  between operations  12.3 us (7%)
  local copies, waits for them, and re-layouts  6.93 us (4%)
    ppermute x8, starting transfers between devices, from_behind(): return lax.ppermute(x, axis, pairs)  35.3 us
    pallas_call x2, Pallas kernels, fused_attention(): pl.pallas_call(functools.partial(far_attention_kernel, final), grid_spec=...  34.8 us
    ppermute x8, waiting for transfers between devices, from_behind(): return lax.ppermute(x, axis, pairs)  27.8 us
    pallas_call x1, Pallas kernels, fused_attention(): pl.pallas_call(own_attention_kernel, grid=(head_count,), in_specs=[pl.Blo...  7.36 us
    dot_general x3, matrix products, per_device(): jnp.dot(arrived, weight_pieces[shift], preferred_element_type=jnp.float32)  6.25 us
    ppermute x3, starting transfers between devices, per_device(): row_pieces.append(lax.ppermute(local_rows, 'tp', pairs))  5.63 us
    ppermute x3, waiting for transfers between devices, per_device(): arrived = lax.ppermute(rows_for((tp_index + shift) % tp_size), 'tp', pairs)  5.53 us
  transfers between devices with their start and end apart: 17, of which 4 were waited for; matrix products, arithmetic and copies ran while one was open for 15% of the time, Pallas kernels for 25%

profile of v1, /device:TPU:1, one launch (start us, length us, event | category | flops | bytes accessed | tf_op | source)
XLA Modules:
  0.0 170.3 jit_solution(3462079052003262327)
XLA Ops:
  0.0 1.3 convert_reduce_fusion.1
  1.4 1.3 fusion.24
  2.7 2.2 %fusion.25 = bf16[128,2048]{1,0:T(8,128)(2,1)} fusion(bf16[128,2048]{1,0:T(8,128)(2,1)} %param.10, f32[128]{0:T(128)S(1)} %add_rsqrt_fusion, f32[128]{0:T(128)S(1)} %broadcast_multiply_fusion), kind=kLoop, calls=%fused_computation.30 | loop fusion | flops 1048576 | bytes 1049600 | tf_op jit(solution)/shard_map/convert_element_type | solution.py:68
  4.9 2.0 %collective-permute-start = (bf16[128,2048]{1,0:T(8,128)(2,1)}, bf16[128,2048]{1,0:T(8,128)(2,1)}, u32[]{:S(2)}, u32[]{:S(2)}) collective-permute-start(bf16[128,2048]{1,0:T(8,128)(2,1)} %fusion.25), channel_id=1, source_target_pairs={{0,1},{1,2},{2,3},{3,0},{4,5},{5,6},{6,7},{7,4},{8,9},{9,10},{10,1... | collective-permute-start | bytes 1572872 | tf_op jit(solution)/shard_map/ppermute | solution.py:249
  6.9 2.5 %collective-permute-start.1 = (bf16[128,2048]{1,0:T(8,128)(2,1)}, bf16[128,2048]{1,0:T(8,128)(2,1)}, u32[]{:S(2)}, u32[]{:S(2)}) collective-permute-start(bf16[128,2048]{1,0:T(8,128)(2,1)} %fusion.25), channel_id=1, source_target_pairs={{0,2},{1,3},{2,0},{3,1},{4,6},{5,7},{6,4},{7,5},{8,10},{9,11},{10,... | collective-permute-start | bytes 1572872 | tf_op jit(solution)/shard_map/ppermute | solution.py:249
  9.4 1.2 collective-permute-start.2
  16.7 2.2 %fusion.19 = bf16[512,1024]{1,0:T(8,128)(2,1)} fusion(bf16[1024,512]{1,0:T(8,128)(2,1)S(1)} %copy-done.16, bf16[1024,512]{1,0:T(8,128)(2,1)S(1)} %fusion.7, s32[1024]{0:T(1024)S(1)} %iota_subtract_fusion, pred[1024]{0:T(1024)(128)(4,1)S(1)} %not.7), kind=kOutput, calls=%fused_computation.24 | convolution fusion | flops 1079508992 | bytes 3150848 | tf_op jit(solution)/shard_map/dot_general | solution.py:236
  19.0 4.7 %collective-permute-start.3 = (bf16[512,1024]{1,0:T(8,128)(2,1)}, bf16[512,1024]{1,0:T(8,128)(2,1)}, u32[]{:S(2)}, u32[]{:S(2)}) collective-permute-start(bf16[512,1024]{1,0:T(8,128)(2,1)} %fusion.19), channel_id=1, source_target_pairs={{0,4},{4,8},{8,12},{12,16},{16,20},{20,24},{24,28},{28,32},{32,36}... | collective-permute-start | bytes 3145736 | tf_op jit(solution)/shard_map/ppermute | solution.py:23
  23.7 4.3 %collective-permute-start.4 = (bf16[512,1024]{1,0:T(8,128)(2,1)}, bf16[512,1024]{1,0:T(8,128)(2,1)}, u32[]{:S(2)}, u32[]{:S(2)}) collective-permute-start(bf16[512,1024]{1,0:T(8,128)(2,1)} %fusion.19), channel_id=1, source_target_pairs={{0,8},{4,12},{8,16},{12,20},{16,24},{20,28},{24,32},{28,36},{32,40... | collective-permute-start | bytes 3145736 | tf_op jit(solution)/shard_map/ppermute | solution.py:23
  30.4 1.9 %collective-permute-start.5 = (bf16[512,1024]{1,0:T(8,128)(2,1)}, bf16[512,1024]{1,0:T(8,128)(2,1)S(1)}, u32[]{:S(2)}, u32[]{:S(2)}) collective-permute-start(bf16[512,1024]{1,0:T(8,128)(2,1)} %fusion.19), channel_id=1, source_target_pairs={{4,0},{8,4},{12,8},{16,12},{20,16},{24,20},{28,24},{32,28},{36,32}... | collective-permute-start | bytes 3145736 | tf_op jit(solution)/shard_map/ppermute | solution.py:23
  32.3 1.5 collective-permute-start.6
  33.8 1.6 pad_maximum_fusion
  35.7 1.2 fusion.34
  37.9 2.3 %fusion.14 = f32[2,512,512]{2,1,0:T(8,128)S(1)} fusion(bf16[2048,2,512]{2,1,0:T(2,128)(2,1)S(1)} %copy-done.15, bf16[128,2048]{1,0:T(8,128)(2,1)S(1)} %get-tuple-element.20, bf16[128,2048]{1,0:T(8,128)(2,1)S(1)} %get-tuple-element.21, bf16[128,2048]{1,0:T(8,128)(2,1)S(1)} %get-tuple-element.22, bf16[128,2048]{1,0:T(8,128)(2,1)S(1)} %get-tuple-element.19), kind=kOutput, calls=%fused_computation.23 | convolution fusion | flops 2155872256 | bytes 8388608 | tf_op jit(solution)/shard_map/nd,dkc->knc/dot_general | solution.py:255
  42.1 1.2 fusion.29
  43.4 1.2 pad_maximum_fusion.4
  44.6 1.3 collective-permute-start.10
  45.9 6.2 %collective-permute-start.7 = (bf16[512,1024]{1,0:T(8,128)(2,1)}, bf16[512,1024]{1,0:T(8,128)(2,1)S(1)}, u32[]{:S(2)}, u32[]{:S(2)}) collective-permute-start(bf16[512,1024]{1,0:T(8,128)(2,1)} %pad_maximum_fusion.4), channel_id=1, source_target_pairs={{0,4},{4,8},{8,12},{12,16},{16,20},{20,24},{24,28},{28,32},{32,36}... | collective-permute-start | bytes 3145736 | tf_op jit(solution)/shard_map/ppermute | solution.py:23
  52.2 6.0 %collective-permute-done.4.refs_2_.refs_3_ = bf16[512,1024]{1,0:T(8,128)(2,1)} collective-permute-done((bf16[512,1024]{1,0:T(8,128)(2,1)}, bf16[512,1024]{1,0:T(8,128)(2,1)}, u32[]{:S(2)}, u32[]{:S(2)}) %collective-permute-start.4) | collective-permute-done | bytes 1048608 | tf_op jit(solution)/shard_map/ppermute | solution.py:23
  59.7 1.3 collective-permute-start.16
  61.0 21.2 %collective-permute-done.10.refs_6_.refs_7_ = bf16[512,1024]{1,0:T(8,128)(2,1)S(1)} collective-permute-done((bf16[512,1024]{1,0:T(8,128)(2,1)}, bf16[512,1024]{1,0:T(8,128)(2,1)S(1)}, u32[]{:S(2)}, u32[]{:S(2)}) %collective-permute-start.10) | collective-permute-done | bytes 1048608 | tf_op jit(solution)/shard_map/ppermute | solution.py:23
  82.2 4.1 %collective-permute-start.8 = (bf16[512,1024]{1,0:T(8,128)(2,1)}, bf16[512,1024]{1,0:T(8,128)(2,1)}, u32[]{:S(2)}, u32[]{:S(2)}) collective-permute-start(bf16[512,1024]{1,0:T(8,128)(2,1)} %pad_maximum_fusion.4), channel_id=1, source_target_pairs={{0,8},{4,12},{8,16},{12,20},{16,24},{20,28},{24,32},{28,36},{32,40... | collective-permute-start | bytes 3145736 | tf_op jit(solution)/shard_map/ppermute | solution.py:23
  86.3 11.3 %collective-permute-start.9 = (bf16[512,1024]{1,0:T(8,128)(2,1)}, bf16[512,1024]{1,0:T(8,128)(2,1)}, u32[]{:S(2)}, u32[]{:S(2)}) collective-permute-start(bf16[512,1024]{1,0:T(8,128)(2,1)} %pad_maximum_fusion.4), channel_id=1, source_target_pairs={{4,0},{8,4},{12,8},{16,12},{20,16},{24,20},{28,24},{32,28},{36,32}... | collective-permute-start | bytes 3145736 | tf_op jit(solution)/shard_map/ppermute | solution.py:23
  108.2 3.0 %convert_select_fusion.own_key_ref.own_value_ref = bf16[1024,1024]{1,0:T(8,128)(2,1)S(1)} fusion(pred[1024]{0:T(1024)(128)(4,1)S(1)} %fusion.10, bf16[1024,512]{1,0:T(8,128)(2,1)} %param.15, bf16[1024,512]{1,0:T(8,128)(2,1)} %copy-done.10, s32[512]{0:T(512)S(1)} %copy-done.12, bf16[512,512]{1,0:T(8,128)(2,1)} %copy-done.8, bf16[512,512]{1,0:T(8,128)(2,1)} %copy-done.9), kind=kOutput, calls=%fused_computation.17 | convolution fusion | flops 1082654720 | bytes 5245952 | tf_op jit(solution)/shard_map/dot_general | solution.py:266
  111.2 7.4 %shard_map.100 = (f32[512,512]{1,0:T(8,128)S(1)}, f32[512,512]{1,0:T(8,128)S(1)}, f32[512,512]{1,0:T(8,128)S(1)}) custom-call(s32[512,1]{1,0:T(8,128)S(1)} %copy.36.index_ref, bf16[512,512]{1,0:T(8,128)(2,1)S(1)} %get-tuple-element.18.query_ref, bf16[1024,1024]{1,0:T(8,128)(2,1)S(1)} %convert_select_fusion.own_key_ref.own_value_ref, ...), custom_call_target="tpu_custom_call" | custom-call | tf_op jit(solution)/shard_map/pallas_call | solution.py:140
  119.7 17.6 %shard_map.101 = (f32[512,512]{1,0:T(8,128)S(1)}, f32[512,512]{1,0:T(8,128)S(1)}, f32[512,512]{1,0:T(8,128)S(1)}) custom-call(s32[4]{0:T(128)S(1)} %add_convert_fusion.1.flags_ref, bf16[512,512]{1,0:T(8,128)(2,1)S(1)} %get-tuple-element.18.query_ref, f32[512,512]{1,0:T(8,128)S(1)} %get-tuple-element.11.max_ref, f32[512,512]{1,0:T(8,128)S(1)} %get-tuple-element.12.sum_ref, ...), custom_call_target="tpu_custom_call" | custom-call | tf_op jit(solution)/shard_map/pallas_call | solution.py:183
  137.3 17.1 %shard_map.102 = bf16[512,512]{1,0:T(8,128)(2,1)S(1)} custom-call(s32[4]{0:T(128)S(1)} %add_convert_fusion.1.flags_ref, bf16[512,512]{1,0:T(8,128)(2,1)S(1)} %get-tuple-element.18.query_ref, f32[512,512]{1,0:T(8,128)S(1)} %get-tuple-element.14.max_ref, f32[512,512]{1,0:T(8,128)S(1)} %get-tuple-element.15.sum_ref, f32[512,512]{1,0:T(8,128)S(1)} %get-tuple-element.16.acc_ref, ...), custom_call_target="tpu_custom_call" | custom-call | tf_op jit(solution)/shard_map/pallas_call | solution.py:183
  155.5 5.5 %collective-permute-done.11 = bf16[128,512]{1,0:T(8,128)(2,1)S(1)} collective-permute-done((bf16[128,512]{1,0:T(8,128)(2,1)S(1)}, bf16[128,512]{1,0:T(8,128)(2,1)S(1)}, u32[]{:S(2)}, u32[]{:S(2)}) %collective-permute-start.11) | collective-permute-done | bytes 131104 | tf_op jit(solution)/shard_map/ppermute | solution.py:292
  161.1 2.0 %fusion.56 = f32[128,2048]{1,0:T(8,128)S(1)} fusion(bf16[128,512]{1,0:T(8,128)(2,1)S(1)} %collective-permute-done.11, bf16[512,2048]{1,0:T(8,128)(2,1)} %collective-permute-done.12), kind=kOutput, calls=%fused_computation.97 | convolution fusion | flops 268435456 | bytes 3276800 | tf_op jit(solution)/shard_map/dot_general | solution.py:293
  163.1 2.0 %fusion.57 = f32[128,2048]{1,0:T(8,128)S(1)} fusion(bf16[128,512]{1,0:T(8,128)(2,1)S(1)} %collective-permute-done.13, bf16[512,2048]{1,0:T(8,128)(2,1)} %collective-permute-done.14), kind=kOutput, calls=%fused_computation.98 | convolution fusion | flops 268435456 | bytes 3276800 | tf_op jit(solution)/shard_map/dot_general | solution.py:293
  165.2 2.2 %fusion.58 = f32[128,2048]{1,0:T(8,128)S(1)} fusion(bf16[128,512]{1,0:T(8,128)(2,1)S(1)} %collective-permute-done.15, bf16[512,2048]{1,0:T(8,128)(2,1)} %collective-permute-done.16), kind=kOutput, calls=%fused_computation.99 | convolution fusion | flops 268435456 | bytes 3276800 | tf_op jit(solution)/shard_map/dot_general | solution.py:293
  167.4 3.0 %fusion.4 = bf16[128,2048]{1,0:T(8,128)(2,1)} fusion(f32[128,2048]{1,0:T(8,128)S(1)} %fusion.58, f32[128,2048]{1,0:T(8,128)S(1)} %fusion.57, f32[128,2048]{1,0:T(8,128)S(1)} %fusion.56, bf16[512,2048]{1,0:T(8,128)(2,1)} %param.13, bf16[512,512]{1,0:T(8,128)(2,1)S(1)} %shard_map.102, s32[]{:T(128)S(6)} %select_n.115), kind=kOutput, calls=%fused_computation.5 | convolution fusion | flops 269484032 | bytes 5898244 | tf_op jit(solution)/shard_map/dot_general | solution.py:289
  (95 shorter events, 14.1 us)
Async XLA Ops:
  0.0 35.7 %copy-start = (bf16[2048,512]{1,0:T(8,128)(2,1)S(1)}, bf16[2048,512]{1,0:T(8,128)(2,1)}, u32[]{:S(2)}) copy-start(bf16[2048,512]{1,0:T(8,128)(2,1)} %param.11) | copy-start | bytes 6291460
  0.0 10.5 %copy-start.14 = (s32[32]{0:T(128)S(1)}, s32[32]{0:T(128)}, u32[]{:S(2)}) copy-start(s32[32]{0:T(128)} %param.16) | copy-start | bytes 388
  0.0 10.9 %copy-start.13 = (s32[64]{0:T(128)S(1)}, s32[64]{0:T(128)}, u32[]{:S(2)}) copy-start(s32[64]{0:T(128)} %param.17) | copy-start | bytes 772
  0.0 11.1 %copy-start.17 = (s32[64]{0:T(128)S(1)}, s32[64]{0:T(128)}, u32[]{:S(2)}) copy-start(s32[64]{0:T(128)} %param.18) | copy-start | bytes 772
  0.0 13.9 %copy-start.3 = (bf16[1024,512]{1,0:T(8,128)(2,1)S(1)}, bf16[1024,512]{1,0:T(8,128)(2,1)}, u32[]{:S(2)}) copy-start(bf16[1024,512]{1,0:T(8,128)(2,1)} %param.14) | copy-start | bytes 3145732
  4.9 25.5 %collective-permute-start = (bf16[128,2048]{1,0:T(8,128)(2,1)}, bf16[128,2048]{1,0:T(8,128)(2,1)}, u32[]{:S(2)}, u32[]{:S(2)}) collective-permute-start(bf16[128,2048]{1,0:T(8,128)(2,1)} %fusion.25), channel_id=1, source_target_pairs={{0,1},{1,2},{2,3},{3,0},{4,5},{5,6},{6,7},{7,4},{8,9},{9,10},{10,1... | collective-permute-start | bytes 1572872 | tf_op jit(solution)/shard_map/ppermute | solution.py:249
  6.9 25.4 %collective-permute-start.1 = (bf16[128,2048]{1,0:T(8,128)(2,1)}, bf16[128,2048]{1,0:T(8,128)(2,1)}, u32[]{:S(2)}, u32[]{:S(2)}) collective-permute-start(bf16[128,2048]{1,0:T(8,128)(2,1)} %fusion.25), channel_id=1, source_target_pairs={{0,2},{1,3},{2,0},{3,1},{4,6},{5,7},{6,4},{7,5},{8,10},{9,11},{10,... | collective-permute-start | bytes 1572872 | tf_op jit(solution)/shard_map/ppermute | solution.py:249
  9.4 24.4 %collective-permute-start.2 = (bf16[128,2048]{1,0:T(8,128)(2,1)}, bf16[128,2048]{1,0:T(8,128)(2,1)}, u32[]{:S(2)}, u32[]{:S(2)}) collective-permute-start(bf16[128,2048]{1,0:T(8,128)(2,1)} %fusion.25), channel_id=1, source_target_pairs={{0,3},{1,0},{2,1},{3,2},{4,7},{5,4},{6,5},{7,6},{8,11},{9,8},{10,9... | collective-permute-start | bytes 1572872 | tf_op jit(solution)/shard_map/ppermute | solution.py:249
  15.5 1.2 copy-start.16
  16.7 2.2 %copy-start.10 = (bf16[1024,512]{1,0:T(8,128)(2,1)}, bf16[1024,512]{1,0:T(8,128)(2,1)S(1)}, u32[]{:S(2)}) copy-start(bf16[1024,512]{1,0:T(8,128)(2,1)S(1)} %fusion.7) | copy-start | bytes 3145732
  19.0 11.1 %copy-start.4 = (bf16[128,2048]{1,0:T(8,128)(2,1)S(1)}, bf16[128,2048]{1,0:T(8,128)(2,1)}, u32[]{:S(2)}) copy-start(bf16[128,2048]{1,0:T(8,128)(2,1)} %param.10) | copy-start | bytes 1572868
  19.0 27.0 %collective-permute-start.3 = (bf16[512,1024]{1,0:T(8,128)(2,1)}, bf16[512,1024]{1,0:T(8,128)(2,1)}, u32[]{:S(2)}, u32[]{:S(2)}) collective-permute-start(bf16[512,1024]{1,0:T(8,128)(2,1)} %fusion.19), channel_id=1, source_target_pairs={{0,4},{4,8},{8,12},{12,16},{16,20},{20,24},{24,28},{28,32},{32,36}... | collective-permute-start | bytes 3145736 | tf_op jit(solution)/shard_map/ppermute | solution.py:23
  23.7 34.5 %collective-permute-start.4 = (bf16[512,1024]{1,0:T(8,128)(2,1)}, bf16[512,1024]{1,0:T(8,128)(2,1)}, u32[]{:S(2)}, u32[]{:S(2)}) collective-permute-start(bf16[512,1024]{1,0:T(8,128)(2,1)} %fusion.19), channel_id=1, source_target_pairs={{0,8},{4,12},{8,16},{12,20},{16,24},{20,28},{24,32},{28,36},{32,40... | collective-permute-start | bytes 3145736 | tf_op jit(solution)/shard_map/ppermute | solution.py:23
  30.4 28.1 %collective-permute-start.5 = (bf16[512,1024]{1,0:T(8,128)(2,1)}, bf16[512,1024]{1,0:T(8,128)(2,1)S(1)}, u32[]{:S(2)}, u32[]{:S(2)}) collective-permute-start(bf16[512,1024]{1,0:T(8,128)(2,1)} %fusion.19), channel_id=1, source_target_pairs={{4,0},{8,4},{12,8},{16,12},{20,16},{24,20},{28,24},{32,28},{36,32}... | collective-permute-start | bytes 3145736 | tf_op jit(solution)/shard_map/ppermute | solution.py:23
  32.3 27.4 %collective-permute-start.6 = (bf16[512,1024]{1,0:T(8,128)(2,1)}, bf16[512,1024]{1,0:T(8,128)(2,1)S(1)}, u32[]{:S(2)}, u32[]{:S(2)}) collective-permute-start(bf16[512,1024]{1,0:T(8,128)(2,1)} %fusion.19), channel_id=1, source_target_pairs={{8,0},{12,4},{16,8},{20,12},{24,16},{28,20},{32,24},{36,28},{40,32... | collective-permute-start | bytes 3145736 | tf_op jit(solution)/shard_map/ppermute | solution.py:23
  35.7 2.2 %copy-start.15 = (bf16[2048,2,512]{2,1,0:T(2,128)(2,1)S(1)}, bf16[2048,2,512]{2,1,0:T(2,128)(2,1)}, u32[]{:S(2)}) copy-start(bf16[2048,2,512]{2,1,0:T(2,128)(2,1)} %param.12) | copy-start | bytes 12582916
  43.3 54.4 %copy-start.9 = (bf16[512,512]{1,0:T(8,128)(2,1)}, bf16[512,512]{1,0:T(8,128)(2,1)S(1)}, u32[]{:S(2)}) copy-start(bf16[512,512]{1,0:T(8,128)(2,1)S(1)} %get-tuple-element.17) | copy-start | bytes 1572868
  43.4 2.5 %copy-start.8 = (bf16[512,512]{1,0:T(8,128)(2,1)}, bf16[512,512]{1,0:T(8,128)(2,1)S(1)}, u32[]{:S(2)}) copy-start(bf16[512,512]{1,0:T(8,128)(2,1)S(1)} %fusion.33) | copy-start | bytes 1572868
  44.6 37.5 %collective-permute-start.10 = (bf16[512,1024]{1,0:T(8,128)(2,1)}, bf16[512,1024]{1,0:T(8,128)(2,1)S(1)}, u32[]{:S(2)}, u32[]{:S(2)}) collective-permute-start(bf16[512,1024]{1,0:T(8,128)(2,1)} %pad_maximum_fusion.4), channel_id=1, source_target_pairs={{8,0},{12,4},{16,8},{20,12},{24,16},{28,20},{32,24},{36,28},{40,32... | collective-permute-start | bytes 3145736 | tf_op jit(solution)/shard_map/ppermute | solution.py:23
  45.9 40.4 %collective-permute-start.7 = (bf16[512,1024]{1,0:T(8,128)(2,1)}, bf16[512,1024]{1,0:T(8,128)(2,1)S(1)}, u32[]{:S(2)}, u32[]{:S(2)}) collective-permute-start(bf16[512,1024]{1,0:T(8,128)(2,1)} %pad_maximum_fusion.4), channel_id=1, source_target_pairs={{0,4},{4,8},{8,12},{12,16},{16,20},{20,24},{24,28},{28,32},{32,36}... | collective-permute-start | bytes 3145736 | tf_op jit(solution)/shard_map/ppermute | solution.py:23
  58.2 102.8 %collective-permute-start.12 = (bf16[512,2048]{1,0:T(8,128)(2,1)}, bf16[512,2048]{1,0:T(8,128)(2,1)}, u32[]{:S(2)}, u32[]{:S(2)}) collective-permute-start(bf16[512,2048]{1,0:T(8,128)(2,1)} %param.13), channel_id=1, source_target_pairs={{0,1},{1,2},{2,3},{3,0},{4,5},{5,6},{6,7},{7,4},{8,9},{9,10},{10,1... | collective-permute-start | bytes 6291464 | tf_op jit(solution)/shard_map/ppermute | solution.py:216
  58.5 52.7 %copy-start.5 = (bf16[512,1024]{1,0:T(8,128)(2,1)}, bf16[512,1024]{1,0:T(8,128)(2,1)S(1)}, u32[]{:S(2)}) copy-start(bf16[512,1024]{1,0:T(8,128)(2,1)S(1)} %collective-permute-done.5.refs_4_.refs_5_) | copy-start | bytes 3145732
  58.5 104.6 %collective-permute-start.14 = (bf16[512,2048]{1,0:T(8,128)(2,1)}, bf16[512,2048]{1,0:T(8,128)(2,1)}, u32[]{:S(2)}, u32[]{:S(2)}) collective-permute-start(bf16[512,2048]{1,0:T(8,128)(2,1)} %param.13), channel_id=1, source_target_pairs={{0,2},{1,3},{2,0},{3,1},{4,6},{5,7},{6,4},{7,5},{8,10},{9,11},{10,... | collective-permute-start | bytes 6291464 | tf_op jit(solution)/shard_map/ppermute | solution.py:216
  59.7 26.6 %copy-start.6 = (bf16[512,1024]{1,0:T(8,128)(2,1)}, bf16[512,1024]{1,0:T(8,128)(2,1)S(1)}, u32[]{:S(2)}) copy-start(bf16[512,1024]{1,0:T(8,128)(2,1)S(1)} %collective-permute-done.6.refs_6_.refs_7_) | copy-start | bytes 3145732
  59.7 105.5 %collective-permute-start.16 = (bf16[512,2048]{1,0:T(8,128)(2,1)}, bf16[512,2048]{1,0:T(8,128)(2,1)}, u32[]{:S(2)}, u32[]{:S(2)}) collective-permute-start(bf16[512,2048]{1,0:T(8,128)(2,1)} %param.13), channel_id=1, source_target_pairs={{0,3},{1,0},{2,1},{3,2},{4,7},{5,4},{6,5},{7,6},{8,11},{9,8},{10,9... | collective-permute-start | bytes 6291464 | tf_op jit(solution)/shard_map/ppermute | solution.py:216
  82.2 4.1 %copy-start.7 = (bf16[512,1024]{1,0:T(8,128)(2,1)}, bf16[512,1024]{1,0:T(8,128)(2,1)S(1)}, u32[]{:S(2)}) copy-start(bf16[512,1024]{1,0:T(8,128)(2,1)S(1)} %collective-permute-done.10.refs_6_.refs_7_) | copy-start | bytes 3145732
  82.2 55.2 %collective-permute-start.8 = (bf16[512,1024]{1,0:T(8,128)(2,1)}, bf16[512,1024]{1,0:T(8,128)(2,1)}, u32[]{:S(2)}, u32[]{:S(2)}) collective-permute-start(bf16[512,1024]{1,0:T(8,128)(2,1)} %pad_maximum_fusion.4), channel_id=1, source_target_pairs={{0,8},{4,12},{8,16},{12,20},{16,24},{20,28},{24,32},{28,36},{32,40... | collective-permute-start | bytes 3145736 | tf_op jit(solution)/shard_map/ppermute | solution.py:23
  86.3 51.0 %collective-permute-start.9 = (bf16[512,1024]{1,0:T(8,128)(2,1)}, bf16[512,1024]{1,0:T(8,128)(2,1)}, u32[]{:S(2)}, u32[]{:S(2)}) collective-permute-start(bf16[512,1024]{1,0:T(8,128)(2,1)} %pad_maximum_fusion.4), channel_id=1, source_target_pairs={{4,0},{8,4},{12,8},{16,12},{20,16},{24,20},{28,24},{32,28},{36,32}... | collective-permute-start | bytes 3145736 | tf_op jit(solution)/shard_map/ppermute | solution.py:23
  154.5 6.5 %collective-permute-start.11 = (bf16[128,512]{1,0:T(8,128)(2,1)S(1)}, bf16[128,512]{1,0:T(8,128)(2,1)S(1)}, u32[]{:S(2)}, u32[]{:S(2)}) collective-permute-start(bf16[128,512]{1,0:T(8,128)(2,1)S(1)} %get-tuple-element.35), channel_id=1, source_target_pairs={{0,1},{1,2},{2,3},{3,0},{4,5},{5,6},{6,7},{7,4},{8,9},{9,10},{10,1... | collective-permute-start | bytes 393224 | tf_op jit(solution)/shard_map/ppermute | solution.py:292
  154.9 8.2 %collective-permute-start.13 = (bf16[128,512]{1,0:T(8,128)(2,1)S(1)}, bf16[128,512]{1,0:T(8,128)(2,1)S(1)}, u32[]{:S(2)}, u32[]{:S(2)}) collective-permute-start(bf16[128,512]{1,0:T(8,128)(2,1)S(1)} %get-tuple-element.37), channel_id=1, source_target_pairs={{0,2},{1,3},{2,0},{3,1},{4,6},{5,7},{6,4},{7,5},{8,10},{9,11},{10,... | collective-permute-start | bytes 393224 | tf_op jit(solution)/shard_map/ppermute | solution.py:292
  161.0 4.1 %collective-permute-start.15 = (bf16[128,512]{1,0:T(8,128)(2,1)S(1)}, bf16[128,512]{1,0:T(8,128)(2,1)S(1)}, u32[]{:S(2)}, u32[]{:S(2)}) collective-permute-start(bf16[128,512]{1,0:T(8,128)(2,1)S(1)} %get-tuple-element.36), channel_id=1, source_target_pairs={{0,3},{1,0},{2,1},{3,2},{4,7},{5,4},{6,5},{7,6},{8,11},{9,8},{10,9... | collective-permute-start | bytes 393224 | tf_op jit(solution)/shard_map/ppermute | solution.py:292
  165.2 5.2 %copy-start.1 = (bf16[2048,512]{1,0:T(8,128)(2,1)S(1)}, bf16[2048,512]{1,0:T(8,128)(2,1)}, u32[]{:S(2)}) copy-start(bf16[2048,512]{1,0:T(8,128)(2,1)} %param.11) | copy-start | bytes 6291460
  (3 other events, 2.8 us)
